TPU v7x, 256 devices: a whole 4x4x8 slice. The times are simulated.
256 devices in a mesh: row: 8 (over x, core), col: 32 (over z, y).
Axes of the slice: x: 4, y: 4, z: 8, core: 2. Of those that a mesh axis runs over, the one named last changes fastest.
Arguments:
- row_points: bfloat16 [512, 64, 256], P('row'), may hold values from -25.5 to 25.5
- col_points: bfloat16 [128, 64, 256], P('col'), may hold values from -25.5 to 25.5
- block_lists: int32 [512, 16], P('row'), may hold values from 0 to 127, as said below
Outputs:
- row_potential: float32 [512, 256], P('row')
- col_potential: float32 [128, 256], P('col')
Inputs may be any that keep to these rules, and one draw needn't show every extreme that they name: `block_lists`: the 16 column blocks of a row block are distinct. Among the row blocks of one index of row, at most 64 list entries name column blocks of one index of col, and exactly 64 for some index of col. Every column block is named by some row block of every index of row.
All inputs are finite; a program needn't handle non-finite values.
Results may differ from a plain program's by a relative error of at most 0.0003.
Values sent between devices are 32-bit elements; how exact they have to be, the bound alone decides.
No kernel may reach another device: no remote copies, remote signals or barrier semaphores. Data moves between devices by JAX's collectives and lax.ppermute only.
A program may use at most 64 MiB of HBM per device.

v0:
```python
import math
import jax
import jax.numpy as jnp
from jax import lax
from jax.sharding import PartitionSpec as P

DIM = 64
ITERS = 4
CAPACITY = 64
eps_reg = 0.05
neg_big = -1e30
group_slots = 8


def tile_partials(
    row_points, col_points, row_norms, col_norms, row_index, col_index, biases, over_columns
):
    row_tiles = row_points[row_index]
    col_tiles = col_points[col_index]
    inner_prod = jnp.einsum(
        "sdp,sdq->spq", row_tiles, col_tiles, preferred_element_type=jnp.float32
    )
    cost_tile = (
        row_norms[row_index][:, :, None] + col_norms[col_index][:, None, :] - 2.0 * inner_prod
    ) / DIM
    if over_columns:
        scores = (biases[:, None, :] - cost_tile) / eps_reg
        reduce_axis = 2
    else:
        scores = (biases[:, :, None] - cost_tile) / eps_reg
        reduce_axis = 1
    peak_vals = jnp.max(scores, axis=reduce_axis)
    totals = jnp.sum(jnp.exp(scores - jnp.expand_dims(peak_vals, reduce_axis)), axis=reduce_axis)
    return (peak_vals, totals)


def slot_partials(
    row_points, col_points, row_norms, col_norms, row_slot, col_slot, biases, over_columns
):
    groups = row_slot.shape[0] // group_slots
    block_size = row_points.shape[2]

    def one_group(members):
        return tile_partials(
            row_points,
            col_points,
            row_norms,
            col_norms,
            members[0],
            members[1],
            members[2],
            over_columns,
        )

    peak_parts, sum_parts = lax.map(
        one_group,
        (
            row_slot.reshape(groups, group_slots),
            col_slot.reshape(groups, group_slots),
            biases.reshape(groups, group_slots, block_size),
        ),
    )
    return (peak_parts.reshape(-1, block_size), sum_parts.reshape(-1, block_size))


def block_combine(peak_parts, sum_parts, members, slot_block, usable):
    block_peak = jnp.max(jnp.where(members[:, :, None], peak_parts[None, :, :], neg_big), axis=1)
    scale = jnp.where(usable[:, None], jnp.exp(peak_parts - block_peak[slot_block]), 0.0)
    block_sum = jnp.dot(
        members.astype(jnp.float32), sum_parts * scale, precision=lax.Precision.HIGHEST
    )
    return (block_peak, block_sum)


def potential_from(peak_vals, totals, log_mass):
    return eps_reg * (log_mass - (peak_vals + jnp.log(totals)))


def body(row_points, col_points, block_lists):
    row_blocks_here = row_points.shape[0]
    col_blocks_here = col_points.shape[0]
    block_size = row_points.shape[2]
    row_mass = -math.log(lax.axis_size("row") * row_blocks_here * block_size)
    col_mass = -math.log(lax.axis_size("col") * col_blocks_here * block_size)
    row_norms = jnp.sum(jnp.square(row_points.astype(jnp.float32)), axis=1)
    col_norms = jnp.sum(jnp.square(col_points.astype(jnp.float32)), axis=1)
    owned = (block_lists // col_blocks_here == lax.axis_index("col")).reshape(-1)
    entry_rank = jnp.cumsum(owned.astype(jnp.int32)) - 1
    slot_list = jnp.arange(CAPACITY, dtype=jnp.int32)
    picked = owned[None, :] & (entry_rank[None, :] == slot_list[:, None])
    entries = jnp.arange(owned.shape[0], dtype=jnp.int32)
    entry_of_slot = jnp.sum(jnp.where(picked, entries[None, :], 0), axis=1)
    usable = jnp.any(picked, axis=1)
    row_slot = entry_of_slot // block_lists.shape[1]
    col_slot = block_lists.reshape(-1)[entry_of_slot] % col_blocks_here
    row_members = (row_slot[None, :] == jnp.arange(row_blocks_here)[:, None]) & usable[None, :]
    col_members = (col_slot[None, :] == jnp.arange(col_blocks_here)[:, None]) & usable[None, :]
    col_potential = jnp.zeros((col_blocks_here, block_size), jnp.float32)
    row_potential = jnp.zeros((row_blocks_here, block_size), jnp.float32)
    for sweep in range(ITERS):
        peak_parts, sum_parts = slot_partials(
            row_points,
            col_points,
            row_norms,
            col_norms,
            row_slot,
            col_slot,
            col_potential[col_slot],
            True,
        )
        block_peak, block_sum = block_combine(peak_parts, sum_parts, row_members, row_slot, usable)
        whole_peak = lax.pmax(block_peak, "col")
        whole_sum = lax.psum(block_sum * jnp.exp(block_peak - whole_peak), "col")
        row_potential = potential_from(whole_peak, whole_sum, row_mass)
        peak_parts, sum_parts = slot_partials(
            row_points,
            col_points,
            row_norms,
            col_norms,
            row_slot,
            col_slot,
            row_potential[row_slot],
            False,
        )
        block_peak, block_sum = block_combine(peak_parts, sum_parts, col_members, col_slot, usable)
        whole_peak = lax.pmax(block_peak, "row")
        whole_sum = lax.psum(block_sum * jnp.exp(block_peak - whole_peak), "row")
        col_potential = potential_from(whole_peak, whole_sum, col_mass)
    return (row_potential, col_potential)


def solution(mesh):
    placed = (P("row", None, None), P("col", None, None), P("row", None))
    return jax.shard_map(
        body,
        mesh=mesh,
        in_specs=placed,
        out_specs=(P("row", None), P("col", None)),
        check_vma=False,
    )
```

profile of v0, /device:TPU:1, one launch (start us, length us, event | category | flops | bytes accessed | tf_op | source)
XLA Modules:
  0.0 1535.6 jit_solution(2969120463154943220)
XLA Ops:
  11.2 2.3 multiply_reduce_fusion
  14.2 32.7 %while.96 = (s32[]{:T(128)}, f32[8,8,256]{2,1,0:T(8,128)S(1)}, f32[8,8,256]{2,1,0:T(8,128)S(1)}, f32[8,8,256]{2,1,0:T(8,128)S(1)}, s32[8,8]{1,0:T(8,128)S(1)}, /...) while((s32[]{:T(128)}, f32[8,8,256]{2,1,0:T(8,128)S(1)}, ...), condition=%wide.region_9.10_spmd, body=%wide.region_6.9_spmd.sunk | while | flops 71825456 | bytes 5906877 | solution.py:55
  46.9 1.8 select_reduce_fusion.3
  48.8 1.5 gather_fusion.34
  50.3 139.6 %all-reduce.9.cloned.1.call-done = f32[64,256]{1,0:T(8,128)} async-done(((f32[64,256]{1,0:T(8,128)}), f32[64,256]{1,0:T(8,128)}) %all-reduce.9.cloned.1.call-update) | async-done | bytes 65552 | tf_op jit(solution)/shard_map/pmax | solution.py:112
  189.9 1.7 convolution_multiply_fusion.3
  191.7 141.8 %all-reduce.11.cloned.1.call-done = f32[64,256]{1,0:T(8,128)} async-done(((f32[64,256]{1,0:T(8,128)}), f32[64,256]{1,0:T(8,128)}) %all-reduce.11.cloned.1.call-update) | async-done | bytes 65552 | tf_op jit(solution)/shard_map/psum | solution.py:113
  335.1 32.8 %while.97 = (s32[]{:T(128)}, f32[8,8,256]{2,1,0:T(8,128)S(1)}, f32[8,8,256]{2,1,0:T(8,128)S(1)}, f32[8,8,256]{2,1,0:T(8,128)S(1)}, s32[8,8]{1,0:T(8,128)S(1)}, /...) while((s32[]{:T(128)}, f32[8,8,256]{2,1,0:T(8,128)S(1)}, ...), condition=%wide.region_16.17_spmd, body=%wide.region_13.16_spmd.sunk | while | flops 71825456 | bytes 5906877 | solution.py:55
  337.5 1.4 fusion.186
  341.6 1.4 fusion.186
  345.7 1.4 fusion.186
  349.8 1.4 fusion.186
  353.9 1.4 fusion.186
  358.0 1.4 fusion.186
  362.2 1.4 fusion.186
  366.3 1.4 fusion.186
  368.8 16.7 %pmax.57 = f32[4,256]{1,0:T(4,128)S(1)} all-reduce(f32[4,256]{1,0:T(4,128)S(1)} %select_reduce_fusion.7), channel_id=1, replica_groups=mesh['row'=8,'col'=32] {'row'}, use_global_device_ids=true, to_apply=%region_18.19 | all-reduce | flops 1024 | bytes 8192 | tf_op jit(solution)/shard_map/pmax | solution.py:126
  385.7 12.4 psum.57
  398.8 32.8 %while.98 = (s32[]{:T(128)}, f32[8,8,256]{2,1,0:T(8,128)S(1)}, f32[8,8,256]{2,1,0:T(8,128)S(1)}, f32[8,8,256]{2,1,0:T(8,128)S(1)}, s32[8,8]{1,0:T(8,128)S(1)}, /...) while((s32[]{:T(128)}, f32[8,8,256]{2,1,0:T(8,128)S(1)}, ...), condition=%wide.region_23.24_spmd, body=%wide.region_20.23_spmd.sunk | while | flops 71825456 | bytes 5906877 | solution.py:55
  401.2 1.4 fusion.191
  405.3 1.4 fusion.191
  431.6 1.8 select_reduce_fusion.2
  433.5 1.5 gather_fusion.38
  435.0 131.6 %all-reduce.13.cloned.1.call-done = f32[64,256]{1,0:T(8,128)} async-done(((f32[64,256]{1,0:T(8,128)}), f32[64,256]{1,0:T(8,128)}) %all-reduce.13.cloned.1.call-update) | async-done | bytes 65552 | tf_op jit(solution)/shard_map/pmax | solution.py:112
  566.6 1.7 convolution_multiply_fusion.2
  568.5 141.7 %all-reduce.15.cloned.1.call-done = f32[64,256]{1,0:T(8,128)} async-done(((f32[64,256]{1,0:T(8,128)}), f32[64,256]{1,0:T(8,128)}) %all-reduce.15.cloned.1.call-update) | async-done | bytes 65552 | tf_op jit(solution)/shard_map/psum | solution.py:113
  711.7 32.8 %while.99 = (s32[]{:T(128)}, f32[8,8,256]{2,1,0:T(8,128)S(1)}, f32[8,8,256]{2,1,0:T(8,128)S(1)}, f32[8,8,256]{2,1,0:T(8,128)S(1)}, s32[8,8]{1,0:T(8,128)S(1)}, /...) while((s32[]{:T(128)}, f32[8,8,256]{2,1,0:T(8,128)S(1)}, ...), condition=%wide.region_30.31_spmd, body=%wide.region_27.30_spmd.sunk | while | flops 71825456 | bytes 5906877 | solution.py:55
  714.1 1.4 fusion.196
  718.2 1.4 fusion.196
  722.3 1.4 fusion.196
  726.4 1.4 fusion.196
  730.5 1.4 fusion.196
  734.6 1.4 fusion.196
  738.7 1.4 fusion.196
  742.8 1.4 fusion.196
  745.4 16.7 %pmax.59 = f32[4,256]{1,0:T(4,128)S(1)} all-reduce(f32[4,256]{1,0:T(4,128)S(1)} %select_reduce_fusion.6), channel_id=1, replica_groups=mesh['row'=8,'col'=32] {'row'}, use_global_device_ids=true, to_apply=%region_32.33 | all-reduce | flops 1024 | bytes 8192 | tf_op jit(solution)/shard_map/pmax | solution.py:126
  762.3 12.4 psum.59
  775.4 32.8 %while.100 = (s32[]{:T(128)}, f32[8,8,256]{2,1,0:T(8,128)S(1)}, f32[8,8,256]{2,1,0:T(8,128)S(1)}, f32[8,8,256]{2,1,0:T(8,128)S(1)}, s32[8,8]{1,0:T(8,128)S(1)}, ...) while((s32[]{:T(128)}, f32[8,8,256]{2,1,0:T(8,128)S(1)}, ...), condition=%wide.region_37.38_spmd, body=%wide.region_34.37_spmd.sunk | while | flops 71825456 | bytes 5906877 | solution.py:55
  808.2 1.8 select_reduce_fusion.1
  810.1 1.5 gather_fusion.42
  811.6 131.6 %all-reduce.17.cloned.1.call-done = f32[64,256]{1,0:T(8,128)} async-done(((f32[64,256]{1,0:T(8,128)}), f32[64,256]{1,0:T(8,128)}) %all-reduce.17.cloned.1.call-update) | async-done | bytes 65552 | tf_op jit(solution)/shard_map/pmax | solution.py:112
  943.2 1.7 convolution_multiply_fusion.1
  945.1 141.7 %all-reduce.19.cloned.1.call-done = f32[64,256]{1,0:T(8,128)} async-done(((f32[64,256]{1,0:T(8,128)}), f32[64,256]{1,0:T(8,128)}) %all-reduce.19.cloned.1.call-update) | async-done | bytes 65552 | tf_op jit(solution)/shard_map/psum | solution.py:113
  1088.3 32.8 %while.101 = (s32[]{:T(128)}, f32[8,8,256]{2,1,0:T(8,128)S(1)}, f32[8,8,256]{2,1,0:T(8,128)S(1)}, f32[8,8,256]{2,1,0:T(8,128)S(1)}, s32[8,8]{1,0:T(8,128)S(1)}, ...) while((s32[]{:T(128)}, f32[8,8,256]{2,1,0:T(8,128)S(1)}, ...), condition=%wide.region_44.45_spmd, body=%wide.region_41.44_spmd.sunk | while | flops 71825456 | bytes 5906877 | solution.py:55
  1090.7 1.4 fusion.206
  1094.8 1.4 fusion.206
  1098.9 1.4 fusion.206
  1103.0 1.4 fusion.206
  1107.1 1.4 fusion.206
  1111.2 1.4 fusion.206
  1115.3 1.4 fusion.206
  1119.4 1.4 fusion.206
  1122.0 16.7 %pmax.61 = f32[4,256]{1,0:T(4,128)S(1)} all-reduce(f32[4,256]{1,0:T(4,128)S(1)} %select_reduce_fusion.5), channel_id=1, replica_groups=mesh['row'=8,'col'=32] {'row'}, use_global_device_ids=true, to_apply=%region_46.47 | all-reduce | flops 1024 | bytes 8192 | tf_op jit(solution)/shard_map/pmax | solution.py:126
  1138.9 12.6 psum.61
  1152.2 32.8 %while.102 = (s32[]{:T(128)}, f32[8,8,256]{2,1,0:T(8,128)S(1)}, f32[8,8,256]{2,1,0:T(8,128)S(1)}, f32[8,8,256]{2,1,0:T(8,128)S(1)}, s32[8,8]{1,0:T(8,128)S(1)}, ...) while((s32[]{:T(128)}, f32[8,8,256]{2,1,0:T(8,128)S(1)}, ...), condition=%wide.region_51.52_spmd, body=%wide.region_48.51_spmd.sunk | while | flops 71825456 | bytes 5906877 | solution.py:55
  1154.6 1.4 fusion.211
  1185.0 1.8 select_reduce_fusion
  1186.9 1.5 gather_fusion.46
  1188.4 131.6 %all-reduce.21.cloned.1.call-done = f32[64,256]{1,0:T(8,128)} async-done(((f32[64,256]{1,0:T(8,128)}), f32[64,256]{1,0:T(8,128)}) %all-reduce.21.cloned.1.call-update) | async-done | bytes 65552 | tf_op jit(solution)/shard_map/pmax | solution.py:112
  1320.0 1.7 convolution_multiply_fusion
  1321.8 141.9 %all-reduce.23.cloned.1.call-done = f32[64,256]{1,0:T(8,128)} async-done(((f32[64,256]{1,0:T(8,128)}), f32[64,256]{1,0:T(8,128)}) %all-reduce.23.cloned.1.call-update) | async-done | bytes 65552 | tf_op jit(solution)/shard_map/psum | solution.py:113
  1465.3 32.7 %while.103 = (s32[]{:T(128)}, f32[8,8,256]{2,1,0:T(8,128)S(1)}, f32[8,8,256]{2,1,0:T(8,128)S(1)}, f32[8,8,256]{2,1,0:T(8,128)S(1)}, s32[8,8]{1,0:T(8,128)S(1)}, ...) while((s32[]{:T(128)}, f32[8,8,256]{2,1,0:T(8,128)S(1)}, ...), condition=%wide.region_58.59_spmd, body=%wide.region_55.58_spmd.sunk | while | flops 71825456 | bytes 5906877 | solution.py:55
  1498.7 16.8 %pmax.63 = f32[4,256]{1,0:T(4,128)S(1)} all-reduce(f32[4,256]{1,0:T(4,128)S(1)} %select_reduce_fusion.4), channel_id=1, replica_groups=mesh['row'=8,'col'=32] {'row'}, use_global_device_ids=true, to_apply=%region_60.61 | all-reduce | flops 1024 | bytes 8192 | tf_op jit(solution)/shard_map/pmax | solution.py:126
  1515.7 12.4 psum.63
  (836 shorter events, 236.3 us)
Async XLA Ops:
  7.2 7.0 copy-start.1
  7.2 6.3 copy-start
  7.2 182.7 %all-reduce.9.cloned.1.call-start = ((), (), s32[]{:S(2)}) async-start(), calls=%async_computation | async-start | bytes 131072 | tf_op jit(solution)/shard_map/pmax | solution.py:112
  48.8 284.8 %all-reduce.11.cloned.1.call-start = ((), (), s32[]{:S(2)}) async-start(), calls=%async_computation.1 | async-start | bytes 131072 | tf_op jit(solution)/shard_map/psum | solution.py:113
  191.7 375.0 %all-reduce.13.cloned.1.call-start = ((), (), s32[]{:S(2)}) async-start(), calls=%async_computation.2 | async-start | bytes 131072 | tf_op jit(solution)/shard_map/pmax | solution.py:112
  433.5 276.7 %all-reduce.15.cloned.1.call-start = ((), (), s32[]{:S(2)}) async-start(), calls=%async_computation.3 | async-start | bytes 131072 | tf_op jit(solution)/shard_map/psum | solution.py:113
  568.4 374.8 %all-reduce.17.cloned.1.call-start = ((), (), s32[]{:S(2)}) async-start(), calls=%async_computation.4 | async-start | bytes 131072 | tf_op jit(solution)/shard_map/pmax | solution.py:112
  810.1 276.7 %all-reduce.19.cloned.1.call-start = ((), (), s32[]{:S(2)}) async-start(), calls=%async_computation.5 | async-start | bytes 131072 | tf_op jit(solution)/shard_map/psum | solution.py:113
  945.0 375.0 %all-reduce.21.cloned.1.call-start = ((), (), s32[]{:S(2)}) async-start(), calls=%async_computation.6 | async-start | bytes 131072 | tf_op jit(solution)/shard_map/pmax | solution.py:112
  1186.8 276.8 %all-reduce.23.cloned.1.call-start = ((), (), s32[]{:S(2)}) async-start(), calls=%async_computation.7 | async-start | bytes 131072 | tf_op jit(solution)/shard_map/psum | solution.py:113
  1464.6 0.7 copy-start.2
Sparse Core Ops, SparseCore 0:
  48.9 140.9 all-reduce.8
  193.9 139.5 all-reduce.10
  433.6 132.9 all-reduce.12
  570.5 139.5 all-reduce.14
  810.2 132.9 all-reduce.16
  947.1 139.5 all-reduce.18
  1187.0 133.0 all-reduce.20
  1324.0 139.5 all-reduce.22
where the time goes:
time: 1540 us
  waiting for transfers between devices  1100 us (71%)
  local copies, waits for them, and re-layouts  162 us (11%)
  blocking collectives  117 us (8%)
  matrix products  97.4 us (6%)
  other arithmetic  37 us (2%)
    psum x4, waiting for transfers between devices, body(): whole_sum = lax.psum(block_sum * jnp.exp(block_peak - whole_peak), 'col')  567 us
    pmax x4, waiting for transfers between devices, body(): whole_peak = lax.pmax(block_peak, 'col')  534 us
    dot_general x64, matrix products, tile_partials(): jnp.einsum('sdp,sdq->spq', row_tiles, col_tiles, preferred_element_type=j...  89.7 us
    pmax x4, blocking collectives, body(): whole_peak = lax.pmax(block_peak, 'row')  67 us
    psum x4, blocking collectives, body(): whole_sum = lax.psum(block_sum * jnp.exp(block_peak - whole_peak), 'row')  49.8 us
    gather x64, local copies, waits for them, and re-layouts, tile_partials(): col_tiles = col_points[col_index]  36.1 us
    gather x64, local copies, waits for them, and re-layouts, tile_partials(): row_tiles = row_points[row_index]  36.1 us
    gather x64, local copies, waits for them, and re-layouts, tile_partials(): row_norms[row_index][:, :, None] + col_norms[col_index][:, None, :]  36 us
  transfers between devices with their start and end apart: 8, of which 8 were waited for; matrix products, arithmetic and copies ran while one was open for 0% of the time, Pallas kernels for 0%

commit v1 on v0

--- a/solution.py
+++ b/solution.py
@@ -124,7 +124,9 @@
         )
         block_peak, block_sum = block_combine(peak_parts, sum_parts, col_members, col_slot, usable)
         whole_peak = lax.pmax(block_peak, "row")
-        whole_sum = lax.psum(block_sum * jnp.exp(block_peak - whole_peak), "row")
+        whole_sum = jnp.sum(
+            lax.all_gather(block_sum * jnp.exp(block_peak - whole_peak), "row"), axis=0
+        )
         col_potential = potential_from(whole_peak, whole_sum, col_mass)
     return (row_potential, col_potential)
 

time: 1540 us -> 1540 us (level)
    all_gather x0 -> x4, blocking collectives: none -> 53.6 us  [body(): lax.all_gather(block_sum * jnp.exp(block_peak - whole_peak), 'row')]
    psum x4 -> x0, blocking collectives: 49.8 us -> none  [body(): whole_sum = lax.psum(block_sum * jnp.exp(block_peak - whole_peak), 'row')]
where the time goes in v1:
time: 1540 us
  waiting for transfers between devices  1100 us (71%)
  local copies, waits for them, and re-layouts  162 us (11%)
  blocking collectives  121 us (8%)
  matrix products  97.5 us (6%)
  other arithmetic  37.1 us (2%)
    psum x4, waiting for transfers between devices, body(): whole_sum = lax.psum(block_sum * jnp.exp(block_peak - whole_peak), 'col')  567 us
    pmax x4, waiting for transfers between devices, body(): whole_peak = lax.pmax(block_peak, 'col')  536 us
    dot_general x64, matrix products, tile_partials(): jnp.einsum('sdp,sdq->spq', row_tiles, col_tiles, preferred_element_type=j...  89.7 us
    pmax x4, blocking collectives, body(): whole_peak = lax.pmax(block_peak, 'row')  67 us
    all_gather x4, blocking collectives, body(): lax.all_gather(block_sum * jnp.exp(block_peak - whole_peak), 'row')  53.6 us
    gather x64, local copies, waits for them, and re-layouts, tile_partials(): row_tiles = row_points[row_index]  36.1 us
    gather x64, local copies, waits for them, and re-layouts, tile_partials(): col_tiles = col_points[col_index]  36.1 us
    gather x64, local copies, waits for them, and re-layouts, tile_partials(): col_norms[col_index][:, None, :]  36 us
  transfers between devices with their start and end apart: 8, of which 8 were waited for; matrix products, arithmetic and copies ran while one was open for 0% of the time, Pallas kernels for 0%

profile of v1, /device:TPU:1, one launch (start us, length us, event | category | flops | bytes accessed | tf_op | source)
XLA Modules:
  0.0 1540.6 jit_solution(5097595745943214700)
XLA Ops:
  11.2 2.3 multiply_reduce_fusion
  14.2 32.7 %while.96 = (s32[]{:T(128)}, f32[8,8,256]{2,1,0:T(8,128)S(1)}, f32[8,8,256]{2,1,0:T(8,128)S(1)}, f32[8,8,256]{2,1,0:T(8,128)S(1)}, s32[8,8]{1,0:T(8,128)S(1)}, /...) while((s32[]{:T(128)}, f32[8,8,256]{2,1,0:T(8,128)S(1)}, ...), condition=%wide.region_9.10_spmd, body=%wide.region_6.9_spmd.sunk | while | flops 71825456 | bytes 5906877 | solution.py:55
  46.9 1.8 select_reduce_fusion.3
  48.8 1.5 gather_fusion.34
  50.3 139.6 %all-reduce.9.cloned.1.call-done = f32[64,256]{1,0:T(8,128)} async-done(((f32[64,256]{1,0:T(8,128)}), f32[64,256]{1,0:T(8,128)}) %all-reduce.9.cloned.1.call-update) | async-done | bytes 65552 | tf_op jit(solution)/shard_map/pmax | solution.py:112
  189.9 1.7 convolution_multiply_fusion.3
  191.7 141.8 %all-reduce.11.cloned.1.call-done = f32[64,256]{1,0:T(8,128)} async-done(((f32[64,256]{1,0:T(8,128)}), f32[64,256]{1,0:T(8,128)}) %all-reduce.11.cloned.1.call-update) | async-done | bytes 65552 | tf_op jit(solution)/shard_map/psum | solution.py:113
  335.1 32.8 %while.97 = (s32[]{:T(128)}, f32[8,8,256]{2,1,0:T(8,128)S(1)}, f32[8,8,256]{2,1,0:T(8,128)S(1)}, f32[8,8,256]{2,1,0:T(8,128)S(1)}, s32[8,8]{1,0:T(8,128)S(1)}, /...) while((s32[]{:T(128)}, f32[8,8,256]{2,1,0:T(8,128)S(1)}, ...), condition=%wide.region_16.17_spmd, body=%wide.region_13.16_spmd.sunk | while | flops 71825456 | bytes 5906877 | solution.py:55
  337.5 1.4 fusion.190
  341.6 1.4 fusion.190
  345.7 1.4 fusion.190
  349.8 1.4 fusion.190
  353.9 1.4 fusion.190
  358.0 1.4 fusion.190
  362.2 1.4 fusion.190
  366.3 1.4 fusion.190
  368.8 16.7 %pmax.57 = f32[4,256]{1,0:T(4,128)S(1)} all-reduce(f32[4,256]{1,0:T(4,128)S(1)} %select_reduce_fusion.7), channel_id=1, replica_groups=mesh['row'=8,'col'=32] {'row'}, use_global_device_ids=true, to_apply=%region_18.19 | all-reduce | flops 1024 | bytes 8192 | tf_op jit(solution)/shard_map/pmax | solution.py:126
  385.7 13.4 all-gather.4
  399.8 32.8 %while.98 = (s32[]{:T(128)}, f32[8,8,256]{2,1,0:T(8,128)S(1)}, f32[8,8,256]{2,1,0:T(8,128)S(1)}, f32[8,8,256]{2,1,0:T(8,128)S(1)}, s32[8,8]{1,0:T(8,128)S(1)}, /...) while((s32[]{:T(128)}, f32[8,8,256]{2,1,0:T(8,128)S(1)}, ...), condition=%wide.region_23.24_spmd, body=%wide.region_20.23_spmd.sunk | while | flops 71825456 | bytes 5906877 | solution.py:55
  432.6 1.8 select_reduce_fusion.2
  434.5 1.5 gather_fusion.38
  436.0 132.0 %all-reduce.13.cloned.1.call-done = f32[64,256]{1,0:T(8,128)} async-done(((f32[64,256]{1,0:T(8,128)}), f32[64,256]{1,0:T(8,128)}) %all-reduce.13.cloned.1.call-update) | async-done | bytes 65552 | tf_op jit(solution)/shard_map/pmax | solution.py:112
  568.1 1.7 convolution_multiply_fusion.2
  569.9 141.7 %all-reduce.15.cloned.1.call-done = f32[64,256]{1,0:T(8,128)} async-done(((f32[64,256]{1,0:T(8,128)}), f32[64,256]{1,0:T(8,128)}) %all-reduce.15.cloned.1.call-update) | async-done | bytes 65552 | tf_op jit(solution)/shard_map/psum | solution.py:113
  713.2 32.8 %while.99 = (s32[]{:T(128)}, f32[8,8,256]{2,1,0:T(8,128)S(1)}, f32[8,8,256]{2,1,0:T(8,128)S(1)}, f32[8,8,256]{2,1,0:T(8,128)S(1)}, s32[8,8]{1,0:T(8,128)S(1)}, /...) while((s32[]{:T(128)}, f32[8,8,256]{2,1,0:T(8,128)S(1)}, ...), condition=%wide.region_30.31_spmd, body=%wide.region_27.30_spmd.sunk | while | flops 71825456 | bytes 5906877 | solution.py:55
  715.5 1.4 fusion.200
  719.6 1.4 fusion.200
  723.7 1.4 fusion.200
  727.8 1.4 fusion.200
  731.9 1.4 fusion.200
  736.0 1.4 fusion.200
  740.2 1.4 fusion.200
  744.3 1.4 fusion.200
  746.8 16.7 %pmax.59 = f32[4,256]{1,0:T(4,128)S(1)} all-reduce(f32[4,256]{1,0:T(4,128)S(1)} %select_reduce_fusion.6), channel_id=1, replica_groups=mesh['row'=8,'col'=32] {'row'}, use_global_device_ids=true, to_apply=%region_32.33 | all-reduce | flops 1024 | bytes 8192 | tf_op jit(solution)/shard_map/pmax | solution.py:126
  763.7 13.4 all-gather.5
  777.8 32.8 %while.100 = (s32[]{:T(128)}, f32[8,8,256]{2,1,0:T(8,128)S(1)}, f32[8,8,256]{2,1,0:T(8,128)S(1)}, f32[8,8,256]{2,1,0:T(8,128)S(1)}, s32[8,8]{1,0:T(8,128)S(1)}, ...) while((s32[]{:T(128)}, f32[8,8,256]{2,1,0:T(8,128)S(1)}, ...), condition=%wide.region_37.38_spmd, body=%wide.region_34.37_spmd.sunk | while | flops 71825456 | bytes 5906877 | solution.py:55
  810.6 1.8 select_reduce_fusion.1
  812.5 1.5 gather_fusion.42
  814.0 132.0 %all-reduce.17.cloned.1.call-done = f32[64,256]{1,0:T(8,128)} async-done(((f32[64,256]{1,0:T(8,128)}), f32[64,256]{1,0:T(8,128)}) %all-reduce.17.cloned.1.call-update) | async-done | bytes 65552 | tf_op jit(solution)/shard_map/pmax | solution.py:112
  946.0 1.7 convolution_multiply_fusion.1
  948.0 141.5 %all-reduce.19.cloned.1.call-done = f32[64,256]{1,0:T(8,128)} async-done(((f32[64,256]{1,0:T(8,128)}), f32[64,256]{1,0:T(8,128)}) %all-reduce.19.cloned.1.call-update) | async-done | bytes 65552 | tf_op jit(solution)/shard_map/psum | solution.py:113
  1091.1 32.8 %while.101 = (s32[]{:T(128)}, f32[8,8,256]{2,1,0:T(8,128)S(1)}, f32[8,8,256]{2,1,0:T(8,128)S(1)}, f32[8,8,256]{2,1,0:T(8,128)S(1)}, s32[8,8]{1,0:T(8,128)S(1)}, ...) while((s32[]{:T(128)}, f32[8,8,256]{2,1,0:T(8,128)S(1)}, ...), condition=%wide.region_44.45_spmd, body=%wide.region_41.44_spmd.sunk | while | flops 71825456 | bytes 5906877 | solution.py:55
  1093.5 1.4 fusion.210
  1097.6 1.4 fusion.210
  1101.7 1.4 fusion.210
  1105.8 1.4 fusion.210
  1109.9 1.4 fusion.210
  1114.0 1.4 fusion.210
  1118.1 1.4 fusion.210
  1122.2 1.4 fusion.210
  1124.8 16.7 %pmax.61 = f32[4,256]{1,0:T(4,128)S(1)} all-reduce(f32[4,256]{1,0:T(4,128)S(1)} %select_reduce_fusion.5), channel_id=1, replica_groups=mesh['row'=8,'col'=32] {'row'}, use_global_device_ids=true, to_apply=%region_46.47 | all-reduce | flops 1024 | bytes 8192 | tf_op jit(solution)/shard_map/pmax | solution.py:126
  1141.7 13.4 all-gather.6
  1155.8 32.8 %while.102 = (s32[]{:T(128)}, f32[8,8,256]{2,1,0:T(8,128)S(1)}, f32[8,8,256]{2,1,0:T(8,128)S(1)}, f32[8,8,256]{2,1,0:T(8,128)S(1)}, s32[8,8]{1,0:T(8,128)S(1)}, ...) while((s32[]{:T(128)}, f32[8,8,256]{2,1,0:T(8,128)S(1)}, ...), condition=%wide.region_51.52_spmd, body=%wide.region_48.51_spmd.sunk | while | flops 71825456 | bytes 5906877 | solution.py:55
  1158.2 1.4 fusion.215
  1162.3 1.4 fusion.215
  1188.6 1.8 select_reduce_fusion
  1190.5 1.5 gather_fusion.46
  1192.0 132.0 %all-reduce.21.cloned.1.call-done = f32[64,256]{1,0:T(8,128)} async-done(((f32[64,256]{1,0:T(8,128)}), f32[64,256]{1,0:T(8,128)}) %all-reduce.21.cloned.1.call-update) | async-done | bytes 65552 | tf_op jit(solution)/shard_map/pmax | solution.py:112
  1324.1 1.7 convolution_multiply_fusion
  1325.8 141.9 %all-reduce.23.cloned.1.call-done = f32[64,256]{1,0:T(8,128)} async-done(((f32[64,256]{1,0:T(8,128)}), f32[64,256]{1,0:T(8,128)}) %all-reduce.23.cloned.1.call-update) | async-done | bytes 65552 | tf_op jit(solution)/shard_map/psum | solution.py:113
  1469.3 32.7 %while.103 = (s32[]{:T(128)}, f32[8,8,256]{2,1,0:T(8,128)S(1)}, f32[8,8,256]{2,1,0:T(8,128)S(1)}, f32[8,8,256]{2,1,0:T(8,128)S(1)}, s32[8,8]{1,0:T(8,128)S(1)}, ...) while((s32[]{:T(128)}, f32[8,8,256]{2,1,0:T(8,128)S(1)}, ...), condition=%wide.region_58.59_spmd, body=%wide.region_55.58_spmd.sunk | while | flops 71825456 | bytes 5906877 | solution.py:55
  1471.7 1.4 fusion.220
  1502.8 16.7 %pmax.63 = f32[4,256]{1,0:T(4,128)S(1)} all-reduce(f32[4,256]{1,0:T(4,128)S(1)} %select_reduce_fusion.4), channel_id=1, replica_groups=mesh['row'=8,'col'=32] {'row'}, use_global_device_ids=true, to_apply=%region_60.61 | all-reduce | flops 1024 | bytes 8192 | tf_op jit(solution)/shard_map/pmax | solution.py:126
  1519.7 13.4 all-gather.7
  (840 shorter events, 236.6 us)
Async XLA Ops:
  7.2 7.0 copy-start.1
  7.2 6.3 copy-start
  7.2 182.7 %all-reduce.9.cloned.1.call-start = ((), (), s32[]{:S(2)}) async-start(), calls=%async_computation | async-start | bytes 131072 | tf_op jit(solution)/shard_map/pmax | solution.py:112
  48.8 284.8 %all-reduce.11.cloned.1.call-start = ((), (), s32[]{:S(2)}) async-start(), calls=%async_computation.1 | async-start | bytes 131072 | tf_op jit(solution)/shard_map/psum | solution.py:113
  191.7 376.4 %all-reduce.13.cloned.1.call-start = ((), (), s32[]{:S(2)}) async-start(), calls=%async_computation.2 | async-start | bytes 131072 | tf_op jit(solution)/shard_map/pmax | solution.py:112
  434.5 277.1 %all-reduce.15.cloned.1.call-start = ((), (), s32[]{:S(2)}) async-start(), calls=%async_computation.3 | async-start | bytes 131072 | tf_op jit(solution)/shard_map/psum | solution.py:113
  569.8 376.2 %all-reduce.17.cloned.1.call-start = ((), (), s32[]{:S(2)}) async-start(), calls=%async_computation.4 | async-start | bytes 131072 | tf_op jit(solution)/shard_map/pmax | solution.py:112
  812.5 277.1 %all-reduce.19.cloned.1.call-start = ((), (), s32[]{:S(2)}) async-start(), calls=%async_computation.5 | async-start | bytes 131072 | tf_op jit(solution)/shard_map/psum | solution.py:113
  947.8 376.2 %all-reduce.21.cloned.1.call-start = ((), (), s32[]{:S(2)}) async-start(), calls=%async_computation.6 | async-start | bytes 131072 | tf_op jit(solution)/shard_map/pmax | solution.py:112
  1190.5 277.2 %all-reduce.23.cloned.1.call-start = ((), (), s32[]{:S(2)}) async-start(), calls=%async_computation.7 | async-start | bytes 131072 | tf_op jit(solution)/shard_map/psum | solution.py:113
  1468.6 0.7 copy-start.2
Sparse Core Ops, SparseCore 0:
  48.9 140.9 all-reduce.8
  193.9 139.5 all-reduce.10
  434.6 133.4 all-reduce.12
  571.9 139.5 all-reduce.14
  812.6 133.3 all-reduce.16
  949.9 139.5 all-reduce.18
  1190.6 133.4 all-reduce.20
  1328.1 139.5 all-reduce.22
